TPU v7x, 512 devices: a whole 4x4x16 slice. The times are simulated.
512 devices in a mesh: aux: 16 (over z), pair: 32 (over y, x, core).
Axes of the slice: x: 4, y: 4, z: 16, core: 2. Of those that a mesh axis runs over, the one named last changes fastest.
Arguments:
- b_tensor: bfloat16 [2560, 262144], P('aux', 'pair'), may hold values from -0.0625 to 0.0625
- eps_occ: float32 [256], replicated, may hold values from -1 to -0.3
- eps_vir: float32 [1024], replicated, may hold values from 0.05 to 3
- trial: bfloat16 [32, 262144], P(None, 'pair'), may hold values from -6 to 6
Outputs:
- trial_next: float32 [32, 262144], P(None, 'pair')
- residual: bfloat16 [32, 262144], P(None, 'pair')
- subspace: float32 [32, 32], replicated
All inputs are finite; a program needn't handle non-finite values.
Results may differ from a plain program's by a relative error of at most 0.028.
Values may be sent and summed in bfloat16 or wider, within the bound.
No kernel may reach another device: no remote copies, remote signals or barrier semaphores. Data moves between devices by JAX's collectives and lax.ppermute only.
A program may use at most 64 MiB of HBM per device.

v0:
```python
import jax
import jax.numpy as jnp
from jax import lax
from jax.sharding import PartitionSpec as P

ITERS = 2
HIGHEST_PRECISION = lax.Precision.HIGHEST


def correlation_of(first_rows, second_rows):
    return lax.dot_general(
        first_rows,
        second_rows,
        (((1,), (1,)), ((), ())),
        precision=HIGHEST_PRECISION,
        preferred_element_type=jnp.float32,
    )


def product(first_mat, second_mat):
    return jnp.dot(
        first_mat, second_mat, precision=HIGHEST_PRECISION, preferred_element_type=jnp.float32
    )


def global_sum(matrices):
    return lax.psum(matrices, "pair")


def orthonormal(trial_now, gram_now):
    lower_tri = jnp.linalg.cholesky(gram_now)
    inverse = lax.linalg.triangular_solve(
        lower_tri, jnp.eye(gram_now.shape[0], dtype=jnp.float32), left_side=True, lower=True
    )
    return product(inverse, trial_now)


def coupling_of(b_tensor, basis_now):
    basis_low = basis_now.astype(jnp.bfloat16)
    partial_proj = lax.dot_general(
        b_tensor, basis_low, (((1,), (1,)), ((), ())), preferred_element_type=jnp.float32
    )
    projected_low = lax.psum(partial_proj, "pair").astype(jnp.bfloat16)
    partial_value = lax.dot_general(
        projected_low, b_tensor, (((0,), (0,)), ((), ())), preferred_element_type=jnp.float32
    )
    return lax.psum(partial_value.astype(jnp.bfloat16), "aux").astype(jnp.float32)


def on_device(b_tensor, eps_occ, eps_vir, trial):
    block_cols = b_tensor.shape[1]
    npair_all = eps_occ.shape[0] * eps_vir.shape[0]
    everything = (eps_vir[None, :] - eps_occ[:, None]).reshape(npair_all)
    diagonal = lax.dynamic_slice_in_dim(everything, lax.axis_index("pair") * block_cols, block_cols)
    trial_now = trial.astype(jnp.float32)
    diag_row = diagonal[None, :]
    for iteration in range(ITERS):
        gram_now = global_sum(correlation_of(trial_now, trial_now) / npair_all)
        basis_now = orthonormal(trial_now, gram_now)
        image_now = coupling_of(b_tensor, basis_now) + diag_row * basis_now
        subspace = global_sum(correlation_of(image_now, basis_now) / npair_all)
        residual = image_now - product(subspace, basis_now)
        trial_now = basis_now - residual / diag_row
    return (trial_now, residual.astype(jnp.bfloat16), subspace)


def solution(mesh):
    in_specs = (P("aux", "pair"), P(), P(), P(None, "pair"))
    out_specs = (P(None, "pair"), P(None, "pair"), P())
    return jax.shard_map(
        on_device, mesh=mesh, in_specs=in_specs, out_specs=out_specs, check_vma=False
    )
```

profile of v0, /device:TPU:32, one launch (start us, length us, event | category | flops | bytes accessed | tf_op | source)
XLA Modules:
  0.0 1066.8 jit_solution(1206010079620472459)
XLA Ops:
  7.2 1.6 convolution_multiply_fusion.3
  8.8 128.4 %psum.56 = f32[32,32]{0,1:T(8,128)S(1)} all-reduce(f32[32,32]{0,1:T(8,128)S(1)} %convolution_multiply_fusion.3), channel_id=1, replica_groups=mesh['aux'=16,'pair'=32] {'pair'}, use_global_device_ids=true, to_apply=%region_0.0 | all-reduce | flops 1024 | bytes 8192 | tf_op jit(solution)/shard_map/psum | solution.py:27
  137.3 2.9 cholesky.44
  140.9 0.7 fusion.12
  141.6 2.4 custom-call.6
  144.2 1.6 fusion.23
  145.9 1.0 copy-done.1
  146.8 0.9 convolution_bitcast_fusion.1
  147.8 123.9 %psum.57 = bf16[160,32]{0,1:T(8,128)(2,1)S(1)} all-reduce(f32[160,32]{0,1:T(8,128)S(1)} %convolution_bitcast_fusion.1), channel_id=1, replica_groups=mesh['aux'=16,'pair'=32] {'pair'}, use_global_device_ids=true, to_apply=%region_3.6 | all-reduce | flops 5120 | bytes 30720 | tf_op jit(solution)/shard_map/psum | solution.py:43
  271.7 1.3 convolution_convert_fusion.1
  273.3 1.2 copy.16
  274.5 0.8 dynamic_slice.3
  275.2 133.4 %all-reduce.3.cloned.1.call-done = bf16[32,8192]{1,0:T(8,128)(2,1)} async-done(((bf16[32,8192]{1,0:T(8,128)(2,1)}), bf16[32,8192]{1,0:T(8,128)(2,1)}) %all-reduce.3.cloned.1.call-update) | async-done | bytes 524304 | tf_op jit(solution)/shard_map/psum | solution.py:47
  408.6 2.9 convolution_multiply_fusion.2
  411.5 123.8 %psum.59 = f32[32,32]{0,1:T(8,128)S(1)} all-reduce(f32[32,32]{0,1:T(8,128)S(1)} %convolution_multiply_fusion.2), channel_id=1, replica_groups=mesh['aux'=16,'pair'=32] {'pair'}, use_global_device_ids=true, to_apply=%region_5.8 | all-reduce | flops 1024 | bytes 8192 | tf_op jit(solution)/shard_map/psum | solution.py:27
  535.3 2.8 fusion.1
  538.1 1.0 copy-done.3
  539.1 1.0 convolution_multiply_fusion.1
  540.0 123.8 %psum.60 = f32[32,32]{0,1:T(8,128)S(1)} all-reduce(f32[32,32]{0,1:T(8,128)S(1)} %convolution_multiply_fusion.1), channel_id=1, replica_groups=mesh['aux'=16,'pair'=32] {'pair'}, use_global_device_ids=true, to_apply=%region_6.9 | all-reduce | flops 1024 | bytes 8192 | tf_op jit(solution)/shard_map/psum | solution.py:27
  663.9 2.9 cholesky.55
  667.5 0.7 fusion.13
  668.1 2.4 custom-call.7
  670.8 2.2 fusion.24
  673.0 1.0 copy-done.2
  674.0 0.9 convolution_bitcast_fusion
  675.0 123.8 %psum.61 = bf16[160,32]{0,1:T(8,128)(2,1)S(1)} all-reduce(f32[160,32]{0,1:T(8,128)S(1)} %convolution_bitcast_fusion), channel_id=1, replica_groups=mesh['aux'=16,'pair'=32] {'pair'}, use_global_device_ids=true, to_apply=%region_7.10 | all-reduce | flops 5120 | bytes 30720 | tf_op jit(solution)/shard_map/psum | solution.py:43
  798.7 1.3 convolution_convert_fusion
  800.1 128.7 %all-reduce.5.cloned.1.call-done = bf16[32,8192]{1,0:T(8,128)(2,1)} async-done(((bf16[32,8192]{1,0:T(8,128)(2,1)}), bf16[32,8192]{1,0:T(8,128)(2,1)}) %all-reduce.5.cloned.1.call-update) | async-done | bytes 524304 | tf_op jit(solution)/shard_map/psum | solution.py:47
  928.9 2.8 convolution_multiply_fusion
  931.7 123.8 %psum.63 = f32[32,32]{0,1:T(8,128)S(1)} all-reduce(f32[32,32]{0,1:T(8,128)S(1)} %convolution_multiply_fusion), channel_id=1, replica_groups=mesh['aux'=16,'pair'=32] {'pair'}, use_global_device_ids=true, to_apply=%region_9.12 | all-reduce | flops 1024 | bytes 8192 | tf_op jit(solution)/shard_map/psum | solution.py:27
  1055.5 0.7 copy.12
  1056.1 3.9 fusion.22
  (28 shorter events, 2.3 us)
Async XLA Ops:
  7.2 139.7 %copy-start = (bf16[160,8192]{1,0:T(8,128)(2,1)S(1)}, bf16[160,8192]{1,0:T(8,128)(2,1)}, u32[]{:S(2)}) copy-start(bf16[160,8192]{1,0:T(8,128)(2,1)} %param.7) | copy-start | bytes 7864324
  7.2 401.5 %all-reduce.3.cloned.1.call-start = ((), (), s32[]{:S(2)}) async-start(), calls=%async_computation | async-start | bytes 1048576 | tf_op jit(solution)/shard_map/psum | solution.py:47
  145.9 1.0 copy-start.1
  147.8 125.4 %copy-start.6 = (f32[1024]{0:T(1024)S(1)}, f32[1024]{0:T(1024)}, u32[]{:S(2)}) copy-start(f32[1024]{0:T(1024)} %param.9) | copy-start | bytes 12292
  147.8 125.3 %copy-start.7 = (f32[256]{0:T(256)S(1)}, f32[256]{0:T(256)}, u32[]{:S(2)}) copy-start(f32[256]{0:T(256)} %param.8) | copy-start | bytes 3076
  273.1 655.8 %all-reduce.5.cloned.1.call-start = ((), (), s32[]{:S(2)}) async-start(), calls=%async_computation.1 | async-start | bytes 1048576 | tf_op jit(solution)/shard_map/psum | solution.py:47
  408.6 126.7 %copy-start.4 = (bf16[32,8192]{1,0:T(8,128)(2,1)S(1)}, bf16[32,8192]{1,0:T(8,128)(2,1)}, u32[]{:S(2)}) copy-start(bf16[32,8192]{1,0:T(8,128)(2,1)} %all-reduce.3.cloned.1.call-done) | copy-start | bytes 1572868
  538.1 1.0 copy-start.3
  673.0 1.0 copy-start.2
  928.9 127.3 %copy-start.5 = (bf16[32,8192]{1,0:T(8,128)(2,1)S(1)}, bf16[32,8192]{1,0:T(8,128)(2,1)}, u32[]{:S(2)}) copy-start(bf16[32,8192]{1,0:T(8,128)(2,1)} %all-reduce.5.cloned.1.call-done) | copy-start | bytes 1572868
Sparse Core Ops, SparseCore 0:
  273.2 135.3 all-reduce.2
  800.2 128.5 all-reduce.4
where the time goes:
time: 1070 us
  blocking collectives  747 us (70%)
  waiting for transfers between devices  262 us (24%)
  matrix products  23.8 us (2%)
  between operations  14.2 us (1%)
  other arithmetic  13.5 us (1%)
    psum x4, blocking collectives, global_sum(): return lax.psum(matrices, 'pair')  500 us
    psum x2, waiting for transfers between devices, coupling_of(): lax.psum(partial_value.astype(jnp.bfloat16), 'aux').astype(jnp.float32)  262 us
    psum x2, blocking collectives, coupling_of(): projected_low = lax.psum(partial_proj, 'pair').astype(jnp.bfloat16)  248 us
  transfers between devices with their start and end apart: 2, of which 2 were waited for; matrix products, arithmetic and copies ran while one was open for 0% of the time, Pallas kernels for 0%

commit v1 on v0

--- a/solution.py
+++ b/solution.py
@@ -24,7 +24,7 @@
 
 
 def global_sum(matrices):
-    return lax.psum(matrices, "pair")
+    return jnp.sum(lax.all_gather(matrices, "pair"), axis=0)
 
 
 def orthonormal(trial_now, gram_now):

time: 1070 us -> 676 us (0.63)
  the two profiles are of different devices: /device:TPU:32 before, /device:TPU:1 now
where the time goes in v1:
time: 676 us; the launch traced here: 675 us
  blocking collectives  367 us (54%)
  waiting for transfers between devices  251 us (37%)
  matrix products  22.9 us (3%)
  other arithmetic  14.8 us (2%)
  between operations  14.2 us (2%)
    psum x2, waiting for transfers between devices, coupling_of(): lax.psum(partial_value.astype(jnp.bfloat16), 'aux').astype(jnp.float32)  251 us
    psum x2, blocking collectives, coupling_of(): projected_low = lax.psum(partial_proj, 'pair').astype(jnp.bfloat16)  242 us
    all_gather x4, blocking collectives, global_sum(): return jnp.sum(lax.all_gather(matrices, 'pair'), axis=0)  125 us
  transfers between devices with their start and end apart: 2, of which 2 were waited for; matrix products, arithmetic and copies ran while one was open for 0% of the time, Pallas kernels for 0%

profile of v1, /device:TPU:1, one launch (start us, length us, event | category | flops | bytes accessed | tf_op | source)
XLA Modules:
  0.0 675.4 jit_solution(4837127541710372627)
XLA Ops:
  7.2 1.6 convolution_multiply_fusion.3
  8.9 31.3 %all-gather = f32[1024,32]{1,0:T(8,128)} all-gather(f32[32,32]{1,0:T(8,128)S(1)} %convolution_multiply_fusion.3), channel_id=2, replica_groups=mesh['aux'=16,'pair'=32] {'pair'}, dimensions={0}, use_global_device_ids=true | all-gather | bytes 135168 | tf_op jit(solution)/shard_map/all_gather | solution.py:27
  40.2 1.1 reduce_sum.36
  41.3 2.9 cholesky.44
  44.9 0.7 fusion.12
  45.6 2.4 custom-call.6
  48.9 1.0 copy-done.1
  49.8 0.9 convolution_bitcast_fusion.1
  50.8 121.0 %psum.28 = bf16[160,32]{0,1:T(8,128)(2,1)S(1)} all-reduce(f32[160,32]{0,1:T(8,128)S(1)} %convolution_bitcast_fusion.1), channel_id=1, replica_groups=mesh['aux'=16,'pair'=32] {'pair'}, use_global_device_ids=true, to_apply=%region_3.6 | all-reduce | flops 5120 | bytes 30720 | tf_op jit(solution)/shard_map/psum | solution.py:43
  171.8 1.3 convolution_convert_fusion.1
  173.4 1.2 copy.11
  174.6 0.8 dynamic_slice.3
  175.3 127.0 %all-reduce.3.cloned.1.call-done = bf16[32,8192]{1,0:T(8,128)(2,1)} async-done(((bf16[32,8192]{1,0:T(8,128)(2,1)}), bf16[32,8192]{1,0:T(8,128)(2,1)}) %all-reduce.3.cloned.1.call-update) | async-done | bytes 524304 | tf_op jit(solution)/shard_map/psum | solution.py:47
  302.4 2.9 convolution_multiply_fusion.2
  305.2 34.8 %all-gather.1 = f32[1024,32]{1,0:T(8,128)S(1)} all-gather(f32[32,32]{1,0:T(8,128)S(1)} %convolution_multiply_fusion.2), channel_id=3, replica_groups=mesh['aux'=16,'pair'=32] {'pair'}, dimensions={0}, use_global_device_ids=true | all-gather | bytes 135168 | tf_op jit(solution)/shard_map/all_gather | solution.py:27
  340.0 2.9 fusion.1
  343.0 1.0 copy-done.3
  343.9 1.0 convolution_multiply_fusion.1
  344.9 24.3 %all-gather.2 = f32[1024,32]{1,0:T(8,128)S(1)} all-gather(f32[32,32]{1,0:T(8,128)S(1)} %convolution_multiply_fusion.1), channel_id=4, replica_groups=mesh['aux'=16,'pair'=32] {'pair'}, dimensions={0}, use_global_device_ids=true | all-gather | bytes 135168 | tf_op jit(solution)/shard_map/all_gather | solution.py:27
  369.3 2.9 cholesky.55
  372.3 0.6 compare_reduce_fusion
  372.9 0.7 fusion.13
  373.6 2.4 custom-call.7
  376.3 2.2 fusion.24
  378.5 1.0 copy-done.2
  379.5 0.9 convolution_bitcast_fusion
  380.4 120.9 %psum.30 = bf16[160,32]{0,1:T(8,128)(2,1)S(1)} all-reduce(f32[160,32]{0,1:T(8,128)S(1)} %convolution_bitcast_fusion), channel_id=1, replica_groups=mesh['aux'=16,'pair'=32] {'pair'}, use_global_device_ids=true, to_apply=%region_7.10 | all-reduce | flops 5120 | bytes 30720 | tf_op jit(solution)/shard_map/psum | solution.py:43
  501.3 1.3 convolution_convert_fusion
  502.7 124.3 %all-reduce.5.cloned.1.call-done = bf16[32,8192]{1,0:T(8,128)(2,1)} async-done(((bf16[32,8192]{1,0:T(8,128)(2,1)}), bf16[32,8192]{1,0:T(8,128)(2,1)}) %all-reduce.5.cloned.1.call-update) | async-done | bytes 524304 | tf_op jit(solution)/shard_map/psum | solution.py:47
  627.0 2.8 convolution_multiply_fusion
  629.8 34.8 %all-gather.3 = f32[1024,32]{1,0:T(8,128)S(1)} all-gather(f32[32,32]{1,0:T(8,128)S(1)} %convolution_multiply_fusion), channel_id=5, replica_groups=mesh['aux'=16,'pair'=32] {'pair'}, dimensions={0}, use_global_device_ids=true | all-gather | bytes 135168 | tf_op jit(solution)/shard_map/all_gather | solution.py:27
  664.6 4.0 fusion.22
  (31 shorter events, 2.4 us)
Async XLA Ops:
  7.2 42.7 %copy-start = (bf16[160,8192]{1,0:T(8,128)(2,1)S(1)}, bf16[160,8192]{1,0:T(8,128)(2,1)}, u32[]{:S(2)}) copy-start(bf16[160,8192]{1,0:T(8,128)(2,1)} %param.7) | copy-start | bytes 7864324
  7.2 41.1 %copy-start.4 = (bf16[32,8192]{1,0:T(8,128)(2,1)S(1)}, bf16[32,8192]{1,0:T(8,128)(2,1)}, u32[]{:S(2)}) copy-start(bf16[32,8192]{1,0:T(8,128)(2,1)} %param.10) | copy-start | bytes 1572868
  7.2 295.2 %all-reduce.3.cloned.1.call-start = ((), (), s32[]{:S(2)}) async-start(), calls=%async_computation | async-start | bytes 1048576 | tf_op jit(solution)/shard_map/psum | solution.py:47
  48.9 1.0 copy-start.1
  50.8 122.4 %copy-start.6 = (f32[1024]{0:T(1024)S(1)}, f32[1024]{0:T(1024)}, u32[]{:S(2)}) copy-start(f32[1024]{0:T(1024)} %param.9) | copy-start | bytes 12292
  50.8 122.4 %copy-start.7 = (f32[256]{0:T(256)S(1)}, f32[256]{0:T(256)}, u32[]{:S(2)}) copy-start(f32[256]{0:T(256)} %param.8) | copy-start | bytes 3076
  173.2 453.8 %all-reduce.5.cloned.1.call-start = ((), (), s32[]{:S(2)}) async-start(), calls=%async_computation.1 | async-start | bytes 1048576 | tf_op jit(solution)/shard_map/psum | solution.py:47
  343.0 1.0 copy-start.3
  378.5 1.0 copy-start.2
  664.6 4.0 copy-start.5
Sparse Core Ops, SparseCore 0:
  173.3 129.0 all-reduce.2
  502.8 124.1 all-reduce.4
